TPU v7x, 512 devices: a whole 4x4x16 slice. The times are simulated.
512 devices in a mesh: context: 64 (over x, z), tensor: 8 (over y, core).
Axes of the slice: x: 4, y: 4, z: 16, core: 2. Of those that a mesh axis runs over, the one named last changes fastest.
Arguments:
- inputs: bfloat16 [8192, 8192], P('context', 'tensor'), may hold values from -0.8984375 to 0.8984375
- grads: bfloat16 [8192, 8192], P('context', 'tensor'), may hold values from -0.8984375 to 0.8984375
- step_size: float32 [128, 8192], P('tensor', 'context'), may hold values from 0.25 to 4
- decay_rate: float32 [128], P('tensor'), may hold values from 0 to 1, as said below
- skip_gain: float32 [128], P('tensor'), may hold values from 0.5 to 1.5
- b_rows: bfloat16 [8192, 128], P(('context', 'tensor')), may hold values from -0.59765625 to 0.59765625
- c_rows: bfloat16 [8192, 128], P(('context', 'tensor')), may hold values from -0.59765625 to 0.59765625
- doc_lengths: int32 [64], replicated, may hold values from 1 to 1536, 8192 in all
Outputs:
- grad_x: float32 [8192, 8192], P('context', 'tensor')
- grad_step: float32 [128, 8192], P('tensor', 'context')
- grad_b: float32 [8192, 128], P(('context', 'tensor'))
- grad_c: float32 [8192, 128], P(('context', 'tensor'))
Inputs may be any that keep to these rules, and one draw needn't show every extreme that they name: doc_lengths sum to 8192; the longest document has exactly 1536 tokens. `decay_rate`: decay rates are positive.
All inputs are finite; a program needn't handle non-finite values.
Results may differ from a plain program's by a relative error of at most 0.0005.
Values may be sent and summed in bfloat16 or wider, within the bound.
No kernel may reach another device: no remote copies, remote signals or barrier semaphores. Data moves between devices by JAX's collectives and lax.ppermute only.
A program may use at most 192 MiB of HBM per device.

v0:
```python
import jax
import jax.numpy as jnp
from jax import lax
from jax.sharding import PartitionSpec as P

HIGH = lax.Precision.HIGHEST


def from_behind(x, axis, by):
    peers = lax.axis_size(axis)
    pairs = [(i, i + by) for i in range(peers) if 0 <= i + by < peers]
    return lax.ppermute(x, axis, pairs)


def local(inputs, grads, step_size, decay_rate, skip_gain, b_rows, c_rows, doc_lengths):
    length = inputs.shape[0]
    heads = step_size.shape[0]
    width = inputs.shape[1] // heads
    rows = lax.all_gather(jnp.stack([b_rows, c_rows]), "tensor", axis=1, tiled=True)
    b_bf, c_bf = (rows[0], rows[1])
    bmat = b_bf.astype(jnp.float32)
    cmat = c_bf.astype(jnp.float32)
    xs = inputs.astype(jnp.float32).reshape(length, heads, width).transpose(1, 0, 2)
    dys = grads.astype(jnp.float32).reshape(length, heads, width).transpose(1, 0, 2)
    offset = lax.axis_index("context") * length
    ends = jnp.cumsum(doc_lengths)
    starts = ends - doc_lengths
    position = offset + jnp.arange(length, dtype=jnp.int32)
    seg = jnp.sum(
        ((starts[None, :] >= offset) & (starts[None, :] <= position[:, None])).astype(jnp.int32),
        axis=1,
    )
    rate = decay_rate[:, None]
    logc = jnp.cumsum(-step_size * rate, axis=1)
    enter = jnp.exp(logc) * (seg == 0).astype(jnp.float32)[None, :]
    leave = jnp.exp(logc[:, -1:] - logc) * (seg == seg[-1]).astype(jnp.float32)[None, :]
    total = enter[:, -1][:, None, None]
    moved = step_size[:, :, None] * xs
    left_u = leave[:, :, None] * moved
    enter_dy = enter[:, :, None] * dys
    local_state = jnp.einsum("hlp,ln->hpn", left_u, bmat, precision=HIGH)
    local_adj = jnp.einsum("hlp,ln->hpn", enter_dy, cmat, precision=HIGH)
    turns = 3 * lax.axis_size("context") // 16
    inc_state = jnp.zeros_like(local_state)
    inc_adj = jnp.zeros_like(local_adj)
    for _ in range(turns):
        send_state, send_adj = lax.optimization_barrier(
            (local_state + total * inc_state, local_adj + total * inc_adj)
        )
        inc_state, inc_adj = lax.optimization_barrier(
            (from_behind(send_state, "context", 1), from_behind(send_adj, "context", -1))
        )
    s_in, g_in = (inc_state, inc_adj)
    index = jnp.arange(length)
    keep = (index[:, None] >= index[None, :]) & (seg[:, None] == seg[None, :])
    weights = jnp.exp(jnp.where(keep[None], logc[:, :, None] - logc[:, None, :], -1e30))
    scores = jnp.dot(c_bf, b_bf.T, preferred_element_type=jnp.float32)
    mixed = weights * scores[None]
    core_loc = jnp.einsum("hij,hip->hjp", mixed, dys, precision=HIGH)
    pairs = jnp.einsum("hip,hjp->hij", dys, moved, precision=HIGH)
    paired = mixed * pairs
    col_total = jnp.sum(paired, axis=1)
    row_total = jnp.sum(paired, axis=2)
    inner = jnp.cumsum(col_total, axis=1) - (jnp.cumsum(row_total, axis=1) - row_total)
    weighted = jnp.sum(weights * pairs, axis=0)
    gb_loc = jnp.dot(weighted.T, cmat, precision=HIGH)
    gc_loc = jnp.dot(weighted, bmat, precision=HIGH)
    b_adj = jnp.einsum("ln,hpn->hlp", bmat, g_in, precision=HIGH)
    c_state = jnp.einsum("ln,hpn->hlp", cmat, s_in, precision=HIGH)
    core = core_loc + leave[:, :, None] * b_adj
    gx = step_size[:, :, None] * core + skip_gain[:, None, None] * dys
    along = jnp.sum(xs * core, axis=2)
    from_state = enter * jnp.einsum(
        "hij,hi->hj", weights, jnp.sum(dys * c_state, axis=2), precision=HIGH
    )
    from_adj = leave * jnp.einsum(
        "hij,hj->hi", weights, jnp.sum(moved * b_adj, axis=2), precision=HIGH
    )
    both = leave * enter * jnp.sum(g_in * s_in, axis=(1, 2))[:, None]
    grad_step = along * (1.0 + rate * step_size) - rate * (inner + from_state + from_adj + both)
    gb = gb_loc + jnp.einsum("hlp,hpn->ln", left_u, g_in, precision=HIGH)
    gc = gc_loc + jnp.einsum("hlp,hpn->ln", enter_dy, s_in, precision=HIGH)
    grad_x = gx.transpose(1, 0, 2).reshape(length, heads * width)
    grad_bc = lax.psum_scatter(jnp.stack([gb, gc]), "tensor", scatter_dimension=1, tiled=True)
    return (grad_x, grad_step, grad_bc[0], grad_bc[1])


def solution(mesh):
    in_specs = (
        P("context", "tensor"),
        P("context", "tensor"),
        P("tensor", "context"),
        P("tensor"),
        P("tensor"),
        P(("context", "tensor"), None),
        P(("context", "tensor"), None),
        P(),
    )
    out_specs = (
        P("context", "tensor"),
        P("tensor", "context"),
        P(("context", "tensor"), None),
        P(("context", "tensor"), None),
    )
    return jax.shard_map(local, mesh=mesh, in_specs=in_specs, out_specs=out_specs, check_vma=False)
```

profile of v0, /device:TPU:2, one launch (start us, length us, event | category | flops | bytes accessed | tf_op | source)
XLA Modules:
  0.0 278.4 jit_solution(14510431676233515382)
XLA Ops:
  10.7 13.3 %all_gather.3 = bf16[2,128,128]{2,1,0:T(8,128)(2,1)S(1)} all-gather(bf16[2,16,128]{2,1,0:T(8,128)(2,1)S(1)} %pad_maximum_fusion.1), channel_id=1, replica_groups=mesh['context'=64,'tensor'=8] {'tensor'}, dimensions={1}, use_global_device_ids=true | all-gather | bytes 73728 | tf_op jit(solution)/shard_map/all_gather | solution.py:19
  26.3 3.8 %collective-permute-start = (f32[16,64,128]{2,1,0:T(8,128)S(1)}, f32[16,64,128]{2,1,0:T(8,128)S(1)}, u32[]{:S(2)}, u32[]{:S(2)}) collective-permute-start(f32[16,64,128]{2,1,0:T(8,128)S(1)} %get-tuple-element.52), channel_id=1, source_target_pairs={{0,8},{8,16},{16,24},{24,32},{32,40},{40,48},{48,56},{56,64},{64,7... | collective-permute-start | bytes 1572872 | tf_op jit(solution)/shard_map/ppermute | solution.py:12
  30.2 9.5 %collective-permute-start.1 = (f32[16,64,128]{2,1,0:T(8,128)S(1)}, f32[16,64,128]{2,1,0:T(8,128)S(1)}, u32[]{:S(2)}, u32[]{:S(2)}) collective-permute-start(f32[16,64,128]{2,1,0:T(8,128)S(1)} %get-tuple-element.53), channel_id=1, source_target_pairs={{8,0},{16,8},{24,16},{32,24},{40,32},{48,40},{56,48},{64,56},{72,6... | collective-permute-start | bytes 1572872 | tf_op jit(solution)/shard_map/ppermute | solution.py:12
  39.6 10.5 %collective-permute-done = f32[16,64,128]{2,1,0:T(8,128)S(1)} collective-permute-done((f32[16,64,128]{2,1,0:T(8,128)S(1)}, f32[16,64,128]{2,1,0:T(8,128)S(1)}, u32[]{:S(2)}, u32[]{:S(2)}) %collective-permute-start) | collective-permute-done | bytes 524320 | tf_op jit(solution)/shard_map/ppermute | solution.py:12
  51.5 1.9 collective-permute-start.2
  53.4 6.5 %collective-permute-start.3 = (f32[16,64,128]{2,1,0:T(8,128)S(1)}, f32[16,64,128]{2,1,0:T(8,128)S(1)}, u32[]{:S(2)}, u32[]{:S(2)}) collective-permute-start(f32[16,64,128]{2,1,0:T(8,128)S(1)} %get-tuple-element.57), channel_id=1, source_target_pairs={{8,0},{16,8},{24,16},{32,24},{40,32},{48,40},{56,48},{64,56},{72,6... | collective-permute-start | bytes 1572872 | tf_op jit(solution)/shard_map/ppermute | solution.py:12
  59.9 9.7 %collective-permute-done.2 = f32[16,64,128]{2,1,0:T(8,128)S(1)} collective-permute-done((f32[16,64,128]{2,1,0:T(8,128)S(1)}, f32[16,64,128]{2,1,0:T(8,128)S(1)}, u32[]{:S(2)}, u32[]{:S(2)}) %collective-permute-start.2) | collective-permute-done | bytes 524320 | tf_op jit(solution)/shard_map/ppermute | solution.py:12
  70.9 1.9 collective-permute-start.4
  72.8 6.5 %collective-permute-start.5 = (f32[16,64,128]{2,1,0:T(8,128)S(1)}, f32[16,64,128]{2,1,0:T(8,128)S(1)}, u32[]{:S(2)}, u32[]{:S(2)}) collective-permute-start(f32[16,64,128]{2,1,0:T(8,128)S(1)} %get-tuple-element.61), channel_id=1, source_target_pairs={{8,0},{16,8},{24,16},{32,24},{40,32},{48,40},{56,48},{64,56},{72,6... | collective-permute-start | bytes 1572872 | tf_op jit(solution)/shard_map/ppermute | solution.py:12
  79.3 8.7 %collective-permute-done.4 = f32[16,64,128]{2,1,0:T(8,128)S(1)} collective-permute-done((f32[16,64,128]{2,1,0:T(8,128)S(1)}, f32[16,64,128]{2,1,0:T(8,128)S(1)}, u32[]{:S(2)}, u32[]{:S(2)}) %collective-permute-start.4) | collective-permute-done | bytes 524320 | tf_op jit(solution)/shard_map/ppermute | solution.py:12
  89.4 1.9 collective-permute-start.6
  91.4 6.5 %collective-permute-start.7 = (f32[16,64,128]{2,1,0:T(8,128)S(1)}, f32[16,64,128]{2,1,0:T(8,128)S(1)}, u32[]{:S(2)}, u32[]{:S(2)}) collective-permute-start(f32[16,64,128]{2,1,0:T(8,128)S(1)} %get-tuple-element.65), channel_id=1, source_target_pairs={{8,0},{16,8},{24,16},{32,24},{40,32},{48,40},{56,48},{64,56},{72,6... | collective-permute-start | bytes 1572872 | tf_op jit(solution)/shard_map/ppermute | solution.py:12
  97.9 7.8 %collective-permute-done.6 = f32[16,64,128]{2,1,0:T(8,128)S(1)} collective-permute-done((f32[16,64,128]{2,1,0:T(8,128)S(1)}, f32[16,64,128]{2,1,0:T(8,128)S(1)}, u32[]{:S(2)}, u32[]{:S(2)}) %collective-permute-start.6) | collective-permute-done | bytes 524320 | tf_op jit(solution)/shard_map/ppermute | solution.py:12
  109.0 6.5 %collective-permute-start.9 = (f32[16,64,128]{2,1,0:T(8,128)S(1)}, f32[16,64,128]{2,1,0:T(8,128)S(1)}, u32[]{:S(2)}, u32[]{:S(2)}) collective-permute-start(f32[16,64,128]{2,1,0:T(8,128)S(1)} %get-tuple-element.69), channel_id=1, source_target_pairs={{8,0},{16,8},{24,16},{32,24},{40,32},{48,40},{56,48},{64,56},{72,6... | collective-permute-start | bytes 1572872 | tf_op jit(solution)/shard_map/ppermute | solution.py:12
  115.5 6.9 %collective-permute-done.8 = f32[16,64,128]{2,1,0:T(8,128)S(1)} collective-permute-done((f32[16,64,128]{2,1,0:T(8,128)S(1)}, f32[16,64,128]{2,1,0:T(8,128)S(1)}, u32[]{:S(2)}, u32[]{:S(2)}) %collective-permute-start.8) | collective-permute-done | bytes 524320 | tf_op jit(solution)/shard_map/ppermute | solution.py:12
  125.7 6.5 %collective-permute-start.11 = (f32[16,64,128]{2,1,0:T(8,128)S(1)}, f32[16,64,128]{2,1,0:T(8,128)S(1)}, u32[]{:S(2)}, u32[]{:S(2)}) collective-permute-start(f32[16,64,128]{2,1,0:T(8,128)S(1)} %get-tuple-element.73), channel_id=1, source_target_pairs={{8,0},{16,8},{24,16},{32,24},{40,32},{48,40},{56,48},{64,56},{72,6... | collective-permute-start | bytes 1572872 | tf_op jit(solution)/shard_map/ppermute | solution.py:12
  132.2 6.0 %collective-permute-done.10 = f32[16,64,128]{2,1,0:T(8,128)S(1)} collective-permute-done((f32[16,64,128]{2,1,0:T(8,128)S(1)}, f32[16,64,128]{2,1,0:T(8,128)S(1)}, u32[]{:S(2)}, u32[]{:S(2)}) %collective-permute-start.10) | collective-permute-done | bytes 524320 | tf_op jit(solution)/shard_map/ppermute | solution.py:12
  141.4 6.5 %collective-permute-start.13 = (f32[16,64,128]{2,1,0:T(8,128)S(1)}, f32[16,64,128]{2,1,0:T(8,128)S(1)}, u32[]{:S(2)}, u32[]{:S(2)}) collective-permute-start(f32[16,64,128]{2,1,0:T(8,128)S(1)} %get-tuple-element.77), channel_id=1, source_target_pairs={{8,0},{16,8},{24,16},{32,24},{40,32},{48,40},{56,48},{64,56},{72,6... | collective-permute-start | bytes 1572872 | tf_op jit(solution)/shard_map/ppermute | solution.py:12
  147.9 5.2 %collective-permute-done.12 = f32[16,64,128]{2,1,0:T(8,128)S(1)} collective-permute-done((f32[16,64,128]{2,1,0:T(8,128)S(1)}, f32[16,64,128]{2,1,0:T(8,128)S(1)}, u32[]{:S(2)}, u32[]{:S(2)}) %collective-permute-start.12) | collective-permute-done | bytes 524320 | tf_op jit(solution)/shard_map/ppermute | solution.py:12
  154.8 1.9 collective-permute-start.14
  156.7 6.5 %collective-permute-start.15 = (f32[16,64,128]{2,1,0:T(8,128)S(1)}, f32[16,64,128]{2,1,0:T(8,128)S(1)}, u32[]{:S(2)}, u32[]{:S(2)}) collective-permute-start(f32[16,64,128]{2,1,0:T(8,128)S(1)} %get-tuple-element.81), channel_id=1, source_target_pairs={{8,0},{16,8},{24,16},{32,24},{40,32},{48,40},{56,48},{64,56},{72,6... | collective-permute-start | bytes 1572872 | tf_op jit(solution)/shard_map/ppermute | solution.py:12
  163.2 5.2 %collective-permute-done.14 = f32[16,64,128]{2,1,0:T(8,128)S(1)} collective-permute-done((f32[16,64,128]{2,1,0:T(8,128)S(1)}, f32[16,64,128]{2,1,0:T(8,128)S(1)}, u32[]{:S(2)}, u32[]{:S(2)}) %collective-permute-start.14) | collective-permute-done | bytes 524320 | tf_op jit(solution)/shard_map/ppermute | solution.py:12
  170.1 1.9 collective-permute-start.16
  172.0 6.5 %collective-permute-start.17 = (f32[16,64,128]{2,1,0:T(8,128)S(1)}, f32[16,64,128]{2,1,0:T(8,128)S(1)}, u32[]{:S(2)}, u32[]{:S(2)}) collective-permute-start(f32[16,64,128]{2,1,0:T(8,128)S(1)} %get-tuple-element.85), channel_id=1, source_target_pairs={{8,0},{16,8},{24,16},{32,24},{40,32},{48,40},{56,48},{64,56},{72,6... | collective-permute-start | bytes 1572872 | tf_op jit(solution)/shard_map/ppermute | solution.py:12
  178.5 5.2 %collective-permute-done.16 = f32[16,64,128]{2,1,0:T(8,128)S(1)} collective-permute-done((f32[16,64,128]{2,1,0:T(8,128)S(1)}, f32[16,64,128]{2,1,0:T(8,128)S(1)}, u32[]{:S(2)}, u32[]{:S(2)}) %collective-permute-start.16) | collective-permute-done | bytes 524320 | tf_op jit(solution)/shard_map/ppermute | solution.py:12
  187.3 6.5 %collective-permute-start.19 = (f32[16,64,128]{2,1,0:T(8,128)S(1)}, f32[16,64,128]{2,1,0:T(8,128)S(1)}, u32[]{:S(2)}, u32[]{:S(2)}) collective-permute-start(f32[16,64,128]{2,1,0:T(8,128)S(1)} %get-tuple-element.89), channel_id=1, source_target_pairs={{8,0},{16,8},{24,16},{32,24},{40,32},{48,40},{56,48},{64,56},{72,6... | collective-permute-start | bytes 1572872 | tf_op jit(solution)/shard_map/ppermute | solution.py:12
  193.8 5.9 %collective-permute-done.18 = f32[16,64,128]{2,1,0:T(8,128)S(1)} collective-permute-done((f32[16,64,128]{2,1,0:T(8,128)S(1)}, f32[16,64,128]{2,1,0:T(8,128)S(1)}, u32[]{:S(2)}, u32[]{:S(2)}) %collective-permute-start.18) | collective-permute-done | bytes 524320 | tf_op jit(solution)/shard_map/ppermute | solution.py:12
  203.5 6.5 %collective-permute-start.21 = (f32[16,64,128]{2,1,0:T(8,128)S(1)}, f32[16,64,128]{2,1,0:T(8,128)S(1)}, u32[]{:S(2)}, u32[]{:S(2)}) collective-permute-start(f32[16,64,128]{2,1,0:T(8,128)S(1)} %get-tuple-element.93), channel_id=1, source_target_pairs={{8,0},{16,8},{24,16},{32,24},{40,32},{48,40},{56,48},{64,56},{72,6... | collective-permute-start | bytes 1572872 | tf_op jit(solution)/shard_map/ppermute | solution.py:12
  212.2 4.7 %collective-permute-done.20 = f32[16,64,128]{2,1,0:T(8,128)S(1)} collective-permute-done((f32[16,64,128]{2,1,0:T(8,128)S(1)}, f32[16,64,128]{2,1,0:T(8,128)S(1)}, u32[]{:S(2)}, u32[]{:S(2)}) %collective-permute-start.20) | collective-permute-done | bytes 524320 | tf_op jit(solution)/shard_map/ppermute | solution.py:12
  218.8 2.1 collective-permute-start.22
  221.0 6.5 %collective-permute-start.23 = (f32[16,64,128]{2,1,0:T(8,128)S(1)}, f32[16,64,128]{2,1,0:T(8,128)S(1)}, u32[]{:S(2)}, u32[]{:S(2)}) collective-permute-start(f32[16,64,128]{2,1,0:T(8,128)S(1)} %get-tuple-element.97), channel_id=1, source_target_pairs={{8,0},{16,8},{24,16},{32,24},{40,32},{48,40},{56,48},{64,56},{72,6... | collective-permute-start | bytes 1572872 | tf_op jit(solution)/shard_map/ppermute | solution.py:12
  244.5 25.7 %reduce-scatter.2.cloned.1.call-done = f32[2,16,128]{2,1,0:T(8,128)} async-done(((f32[2,128,128]{2,1,0:T(8,128)}), f32[2,16,128]{2,1,0:T(8,128)}) %reduce-scatter.2.cloned.1.call-update) | async-done | bytes 16400 | tf_op jit(solution)/shard_map/reduce_scatter | solution.py:84
  (116 shorter events, 52.5 us)
Async XLA Ops:
  7.2 263.0 %reduce-scatter.2.cloned.1.call-start = ((), (), s32[]{:S(2)}) async-start(), calls=%async_computation.1 | async-start | bytes 147456 | tf_op jit(solution)/shard_map/reduce_scatter | solution.py:84
  8.2 1.4 copy-start
  10.0 200.3 %copy-start.5 = (f32[16,128]{1,0:T(8,128)}, f32[16,128]{1,0:T(8,128)S(1)}, u32[]{:S(2)}) copy-start(f32[16,128]{1,0:T(8,128)S(1)} %reduce_window_sum.30) | copy-start | bytes 24580
  23.9 1.4 copy-start.1
  26.3 23.8 %collective-permute-start = (f32[16,64,128]{2,1,0:T(8,128)S(1)}, f32[16,64,128]{2,1,0:T(8,128)S(1)}, u32[]{:S(2)}, u32[]{:S(2)}) collective-permute-start(f32[16,64,128]{2,1,0:T(8,128)S(1)} %get-tuple-element.52), channel_id=1, source_target_pairs={{0,8},{8,16},{16,24},{24,32},{32,40},{40,48},{48,56},{56,64},{64,7... | collective-permute-start | bytes 1572872 | tf_op jit(solution)/shard_map/ppermute | solution.py:12
  30.2 21.1 %collective-permute-start.1 = (f32[16,64,128]{2,1,0:T(8,128)S(1)}, f32[16,64,128]{2,1,0:T(8,128)S(1)}, u32[]{:S(2)}, u32[]{:S(2)}) collective-permute-start(f32[16,64,128]{2,1,0:T(8,128)S(1)} %get-tuple-element.53), channel_id=1, source_target_pairs={{8,0},{16,8},{24,16},{32,24},{40,32},{48,40},{56,48},{64,56},{72,6... | collective-permute-start | bytes 1572872 | tf_op jit(solution)/shard_map/ppermute | solution.py:12
  51.5 18.1 %collective-permute-start.2 = (f32[16,64,128]{2,1,0:T(8,128)S(1)}, f32[16,64,128]{2,1,0:T(8,128)S(1)}, u32[]{:S(2)}, u32[]{:S(2)}) collective-permute-start(f32[16,64,128]{2,1,0:T(8,128)S(1)} %get-tuple-element.56), channel_id=1, source_target_pairs={{0,8},{8,16},{16,24},{24,32},{32,40},{40,48},{48,56},{56,64},{64,7... | collective-permute-start | bytes 1572872 | tf_op jit(solution)/shard_map/ppermute | solution.py:12
  53.4 17.3 %collective-permute-start.3 = (f32[16,64,128]{2,1,0:T(8,128)S(1)}, f32[16,64,128]{2,1,0:T(8,128)S(1)}, u32[]{:S(2)}, u32[]{:S(2)}) collective-permute-start(f32[16,64,128]{2,1,0:T(8,128)S(1)} %get-tuple-element.57), channel_id=1, source_target_pairs={{8,0},{16,8},{24,16},{32,24},{40,32},{48,40},{56,48},{64,56},{72,6... | collective-permute-start | bytes 1572872 | tf_op jit(solution)/shard_map/ppermute | solution.py:12
  70.9 17.2 %collective-permute-start.4 = (f32[16,64,128]{2,1,0:T(8,128)S(1)}, f32[16,64,128]{2,1,0:T(8,128)S(1)}, u32[]{:S(2)}, u32[]{:S(2)}) collective-permute-start(f32[16,64,128]{2,1,0:T(8,128)S(1)} %get-tuple-element.60), channel_id=1, source_target_pairs={{0,8},{8,16},{16,24},{24,32},{32,40},{40,48},{48,56},{56,64},{64,7... | collective-permute-start | bytes 1572872 | tf_op jit(solution)/shard_map/ppermute | solution.py:12
  72.8 16.4 %collective-permute-start.5 = (f32[16,64,128]{2,1,0:T(8,128)S(1)}, f32[16,64,128]{2,1,0:T(8,128)S(1)}, u32[]{:S(2)}, u32[]{:S(2)}) collective-permute-start(f32[16,64,128]{2,1,0:T(8,128)S(1)} %get-tuple-element.61), channel_id=1, source_target_pairs={{8,0},{16,8},{24,16},{32,24},{40,32},{48,40},{56,48},{64,56},{72,6... | collective-permute-start | bytes 1572872 | tf_op jit(solution)/shard_map/ppermute | solution.py:12
  89.4 16.3 %collective-permute-start.6 = (f32[16,64,128]{2,1,0:T(8,128)S(1)}, f32[16,64,128]{2,1,0:T(8,128)S(1)}, u32[]{:S(2)}, u32[]{:S(2)}) collective-permute-start(f32[16,64,128]{2,1,0:T(8,128)S(1)} %get-tuple-element.64), channel_id=1, source_target_pairs={{0,8},{8,16},{16,24},{24,32},{32,40},{40,48},{48,56},{56,64},{64,7... | collective-permute-start | bytes 1572872 | tf_op jit(solution)/shard_map/ppermute | solution.py:12
  91.4 15.5 %collective-permute-start.7 = (f32[16,64,128]{2,1,0:T(8,128)S(1)}, f32[16,64,128]{2,1,0:T(8,128)S(1)}, u32[]{:S(2)}, u32[]{:S(2)}) collective-permute-start(f32[16,64,128]{2,1,0:T(8,128)S(1)} %get-tuple-element.65), channel_id=1, source_target_pairs={{8,0},{16,8},{24,16},{32,24},{40,32},{48,40},{56,48},{64,56},{72,6... | collective-permute-start | bytes 1572872 | tf_op jit(solution)/shard_map/ppermute | solution.py:12
  107.0 15.3 %collective-permute-start.8 = (f32[16,64,128]{2,1,0:T(8,128)S(1)}, f32[16,64,128]{2,1,0:T(8,128)S(1)}, u32[]{:S(2)}, u32[]{:S(2)}) collective-permute-start(f32[16,64,128]{2,1,0:T(8,128)S(1)} %get-tuple-element.68), channel_id=1, source_target_pairs={{0,8},{8,16},{16,24},{24,32},{32,40},{40,48},{48,56},{56,64},{64,7... | collective-permute-start | bytes 1572872 | tf_op jit(solution)/shard_map/ppermute | solution.py:12
  109.0 14.6 %collective-permute-start.9 = (f32[16,64,128]{2,1,0:T(8,128)S(1)}, f32[16,64,128]{2,1,0:T(8,128)S(1)}, u32[]{:S(2)}, u32[]{:S(2)}) collective-permute-start(f32[16,64,128]{2,1,0:T(8,128)S(1)} %get-tuple-element.69), channel_id=1, source_target_pairs={{8,0},{16,8},{24,16},{32,24},{40,32},{48,40},{56,48},{64,56},{72,6... | collective-permute-start | bytes 1572872 | tf_op jit(solution)/shard_map/ppermute | solution.py:12
  123.7 14.4 %collective-permute-start.10 = (f32[16,64,128]{2,1,0:T(8,128)S(1)}, f32[16,64,128]{2,1,0:T(8,128)S(1)}, u32[]{:S(2)}, u32[]{:S(2)}) collective-permute-start(f32[16,64,128]{2,1,0:T(8,128)S(1)} %get-tuple-element.72), channel_id=1, source_target_pairs={{0,8},{8,16},{16,24},{24,32},{32,40},{40,48},{48,56},{56,64},{64,7... | collective-permute-start | bytes 1572872 | tf_op jit(solution)/shard_map/ppermute | solution.py:12
  125.7 13.7 %collective-permute-start.11 = (f32[16,64,128]{2,1,0:T(8,128)S(1)}, f32[16,64,128]{2,1,0:T(8,128)S(1)}, u32[]{:S(2)}, u32[]{:S(2)}) collective-permute-start(f32[16,64,128]{2,1,0:T(8,128)S(1)} %get-tuple-element.73), channel_id=1, source_target_pairs={{8,0},{16,8},{24,16},{32,24},{40,32},{48,40},{56,48},{64,56},{72,6... | collective-permute-start | bytes 1572872 | tf_op jit(solution)/shard_map/ppermute | solution.py:12
  139.5 13.7 %collective-permute-start.12 = (f32[16,64,128]{2,1,0:T(8,128)S(1)}, f32[16,64,128]{2,1,0:T(8,128)S(1)}, u32[]{:S(2)}, u32[]{:S(2)}) collective-permute-start(f32[16,64,128]{2,1,0:T(8,128)S(1)} %get-tuple-element.76), channel_id=1, source_target_pairs={{0,8},{8,16},{16,24},{24,32},{32,40},{40,48},{48,56},{56,64},{64,7... | collective-permute-start | bytes 1572872 | tf_op jit(solution)/shard_map/ppermute | solution.py:12
  141.4 13.2 %collective-permute-start.13 = (f32[16,64,128]{2,1,0:T(8,128)S(1)}, f32[16,64,128]{2,1,0:T(8,128)S(1)}, u32[]{:S(2)}, u32[]{:S(2)}) collective-permute-start(f32[16,64,128]{2,1,0:T(8,128)S(1)} %get-tuple-element.77), channel_id=1, source_target_pairs={{8,0},{16,8},{24,16},{32,24},{40,32},{48,40},{56,48},{64,56},{72,6... | collective-permute-start | bytes 1572872 | tf_op jit(solution)/shard_map/ppermute | solution.py:12
  154.8 13.7 %collective-permute-start.14 = (f32[16,64,128]{2,1,0:T(8,128)S(1)}, f32[16,64,128]{2,1,0:T(8,128)S(1)}, u32[]{:S(2)}, u32[]{:S(2)}) collective-permute-start(f32[16,64,128]{2,1,0:T(8,128)S(1)} %get-tuple-element.80), channel_id=1, source_target_pairs={{0,8},{8,16},{16,24},{24,32},{32,40},{40,48},{48,56},{56,64},{64,7... | collective-permute-start | bytes 1572872 | tf_op jit(solution)/shard_map/ppermute | solution.py:12
  156.7 13.2 %collective-permute-start.15 = (f32[16,64,128]{2,1,0:T(8,128)S(1)}, f32[16,64,128]{2,1,0:T(8,128)S(1)}, u32[]{:S(2)}, u32[]{:S(2)}) collective-permute-start(f32[16,64,128]{2,1,0:T(8,128)S(1)} %get-tuple-element.81), channel_id=1, source_target_pairs={{8,0},{16,8},{24,16},{32,24},{40,32},{48,40},{56,48},{64,56},{72,6... | collective-permute-start | bytes 1572872 | tf_op jit(solution)/shard_map/ppermute | solution.py:12
  170.1 13.7 %collective-permute-start.16 = (f32[16,64,128]{2,1,0:T(8,128)S(1)}, f32[16,64,128]{2,1,0:T(8,128)S(1)}, u32[]{:S(2)}, u32[]{:S(2)}) collective-permute-start(f32[16,64,128]{2,1,0:T(8,128)S(1)} %get-tuple-element.84), channel_id=1, source_target_pairs={{0,8},{8,16},{16,24},{24,32},{32,40},{40,48},{48,56},{56,64},{64,7... | collective-permute-start | bytes 1572872 | tf_op jit(solution)/shard_map/ppermute | solution.py:12
  172.0 13.2 %collective-permute-start.17 = (f32[16,64,128]{2,1,0:T(8,128)S(1)}, f32[16,64,128]{2,1,0:T(8,128)S(1)}, u32[]{:S(2)}, u32[]{:S(2)}) collective-permute-start(f32[16,64,128]{2,1,0:T(8,128)S(1)} %get-tuple-element.85), channel_id=1, source_target_pairs={{8,0},{16,8},{24,16},{32,24},{40,32},{48,40},{56,48},{64,56},{72,6... | collective-permute-start | bytes 1572872 | tf_op jit(solution)/shard_map/ppermute | solution.py:12
  185.3 14.3 %collective-permute-start.18 = (f32[16,64,128]{2,1,0:T(8,128)S(1)}, f32[16,64,128]{2,1,0:T(8,128)S(1)}, u32[]{:S(2)}, u32[]{:S(2)}) collective-permute-start(f32[16,64,128]{2,1,0:T(8,128)S(1)} %get-tuple-element.88), channel_id=1, source_target_pairs={{0,8},{8,16},{16,24},{24,32},{32,40},{40,48},{48,56},{56,64},{64,7... | collective-permute-start | bytes 1572872 | tf_op jit(solution)/shard_map/ppermute | solution.py:12
  187.3 14.1 %collective-permute-start.19 = (f32[16,64,128]{2,1,0:T(8,128)S(1)}, f32[16,64,128]{2,1,0:T(8,128)S(1)}, u32[]{:S(2)}, u32[]{:S(2)}) collective-permute-start(f32[16,64,128]{2,1,0:T(8,128)S(1)} %get-tuple-element.89), channel_id=1, source_target_pairs={{8,0},{16,8},{24,16},{32,24},{40,32},{48,40},{56,48},{64,56},{72,6... | collective-permute-start | bytes 1572872 | tf_op jit(solution)/shard_map/ppermute | solution.py:12
  201.6 15.4 %collective-permute-start.20 = (f32[16,64,128]{2,1,0:T(8,128)S(1)}, f32[16,64,128]{2,1,0:T(8,128)S(1)}, u32[]{:S(2)}, u32[]{:S(2)}) collective-permute-start(f32[16,64,128]{2,1,0:T(8,128)S(1)} %get-tuple-element.92), channel_id=1, source_target_pairs={{0,8},{8,16},{16,24},{24,32},{32,40},{40,48},{48,56},{56,64},{64,7... | collective-permute-start | bytes 1572872 | tf_op jit(solution)/shard_map/ppermute | solution.py:12
  203.5 15.2 %collective-permute-start.21 = (f32[16,64,128]{2,1,0:T(8,128)S(1)}, f32[16,64,128]{2,1,0:T(8,128)S(1)}, u32[]{:S(2)}, u32[]{:S(2)}) collective-permute-start(f32[16,64,128]{2,1,0:T(8,128)S(1)} %get-tuple-element.93), channel_id=1, source_target_pairs={{8,0},{16,8},{24,16},{32,24},{40,32},{48,40},{56,48},{64,56},{72,6... | collective-permute-start | bytes 1572872 | tf_op jit(solution)/shard_map/ppermute | solution.py:12
  210.2 2.0 copy-start.8
  212.2 15.4 %copy-start.10 = (f32[16,128]{1,0:T(8,128)}, f32[16,128]{1,0:T(8,128)S(1)}, u32[]{:S(2)}) copy-start(f32[16,128]{1,0:T(8,128)S(1)} %get-tuple-element.116) | copy-start | bytes 24580
  218.8 13.7 %collective-permute-start.22 = (f32[16,64,128]{2,1,0:T(8,128)S(1)}, f32[16,64,128]{2,1,0:T(8,128)S(1)}, u32[]{:S(2)}, u32[]{:S(2)}) collective-permute-start(f32[16,64,128]{2,1,0:T(8,128)S(1)} %get-tuple-element.96), channel_id=1, source_target_pairs={{0,8},{8,16},{16,24},{24,32},{32,40},{40,48},{48,56},{56,64},{64,7... | collective-permute-start | bytes 1572872 | tf_op jit(solution)/shard_map/ppermute | solution.py:12
  221.0 13.0 %collective-permute-start.23 = (f32[16,64,128]{2,1,0:T(8,128)S(1)}, f32[16,64,128]{2,1,0:T(8,128)S(1)}, u32[]{:S(2)}, u32[]{:S(2)}) collective-permute-start(f32[16,64,128]{2,1,0:T(8,128)S(1)} %get-tuple-element.97), channel_id=1, source_target_pairs={{8,0},{16,8},{24,16},{32,24},{40,32},{48,40},{56,48},{64,56},{72,6... | collective-permute-start | bytes 1572872 | tf_op jit(solution)/shard_map/ppermute | solution.py:12
  231.6 2.8 copy-start.3
  242.2 1.0 copy-start.12
  (16 other events, 12.3 us)
Sparse Core Ops, SparseCore 0:
  237.2 32.9 reduce-scatter.1
where the time goes:
time: 280 us; the launch traced here: 278 us
  waiting for transfers between devices  119 us (42%)
  starting transfers between devices  106 us (38%)
  between operations  14.6 us (5%)
  blocking collectives  13.3 us (5%)
  matrix products  10.1 us (4%)
  local copies, waits for them, and re-layouts  8.7 us (3%)
  other arithmetic  6.84 us (2%)
    ppermute x24, starting transfers between devices, from_behind(): return lax.ppermute(x, axis, pairs)  106 us
    ppermute x24, waiting for transfers between devices, from_behind(): return lax.ppermute(x, axis, pairs)  93.1 us
    reduce_scatter x1, waiting for transfers between devices, local(): lax.psum_scatter(jnp.stack([gb, gc]), 'tensor', scatter_dimension=1, tile...  25.7 us
    all_gather x1, blocking collectives, local(): lax.all_gather(jnp.stack([b_rows, c_rows]), 'tensor', axis=1, tiled=True)  13.3 us
  transfers between devices with their start and end apart: 25, of which 25 were waited for; matrix products, arithmetic and copies ran while one was open for 4% of the time, Pallas kernels for 0%

commit v1 on v0

--- a/solution.py
+++ b/solution.py
@@ -16,7 +16,12 @@
     length = inputs.shape[0]
     heads = step_size.shape[0]
     width = inputs.shape[1] // heads
-    rows = lax.all_gather(jnp.stack([b_rows, c_rows]), "tensor", axis=1, tiled=True)
+    rows = jnp.concatenate(
+        lax.all_to_all(
+            jnp.stack([jnp.stack([b_rows, c_rows])] * lax.axis_size("tensor")), "tensor", 0, 0
+        ),
+        axis=1,
+    )
     b_bf, c_bf = (rows[0], rows[1])
     bmat = b_bf.astype(jnp.float32)
     cmat = c_bf.astype(jnp.float32)

time: 280 us -> 272 us (0.971)
  blocking collectives: 13.3 us -> 0 us
  starting transfers between devices: 106 us -> 111 us
  waiting for transfers between devices: 119 us -> 122 us
    all_gather x1 -> x0, blocking collectives: 13.3 us -> none  [local(): lax.all_gather(jnp.stack([b_rows, c_rows]), 'tensor', axis=1, tiled=True)]
    all_to_all x0 -> x1, starting transfers between devices: none -> 4.47 us  [local(): lax.all_to_all(jnp.stack([jnp.stack([b_rows, c_rows])] * lax.axis_size('t...]
  transfers between devices with their start and end apart: 25 -> 26, of which waited for: 25 -> 26; matrix products, arithmetic and copies ran while one was open for 4% -> 5% of each run, Pallas kernels for 0% -> 0%
where the time goes in v1:
time: 272 us; the launch traced here: 271 us
  waiting for transfers between devices  122 us (45%)
  starting transfers between devices  111 us (41%)
  between operations  14.5 us (5%)
  matrix products  10.1 us (4%)
  other arithmetic  7.2 us (3%)
  local copies, waits for them, and re-layouts  6.95 us (3%)
    ppermute x24, starting transfers between devices, from_behind(): return lax.ppermute(x, axis, pairs)  106 us
    ppermute x24, waiting for transfers between devices, from_behind(): return lax.ppermute(x, axis, pairs)  93.2 us
    reduce_scatter x1, waiting for transfers between devices, local(): lax.psum_scatter(jnp.stack([gb, gc]), 'tensor', scatter_dimension=1, tile...  27.7 us
  transfers between devices with their start and end apart: 26, of which 26 were waited for; matrix products, arithmetic and copies ran while one was open for 5% of the time, Pallas kernels for 0%

profile of v1, /device:TPU:2, one launch (start us, length us, event | category | flops | bytes accessed | tf_op | source)
XLA Modules:
  0.0 271.0 jit_solution(12189318835786711779)
XLA Ops:
  8.6 4.5 %all-to-all-start = ((bf16[8,2,16,128]{3,2,1,0:T(8,128)(2,1)}), bf16[8,2,16,128]{3,2,1,0:T(8,128)(2,1)S(1)}, u32[]{:S(2)}, u32[]{:S(2)}) async-start(bf16[8,2,16,128]{3,2,1,0:T(8,128)(2,1)} %stack.32), calls=%async_computation | async-start | bytes 131072 | tf_op jit(solution)/shard_map/all_to_all | solution.py:20
  19.5 3.8 %collective-permute-start = (f32[16,64,128]{2,1,0:T(8,128)S(1)}, f32[16,64,128]{2,1,0:T(8,128)S(1)}, u32[]{:S(2)}, u32[]{:S(2)}) collective-permute-start(f32[16,64,128]{2,1,0:T(8,128)S(1)} %get-tuple-element.52), channel_id=1, source_target_pairs={{0,8},{8,16},{16,24},{24,32},{32,40},{40,48},{48,56},{56,64},{64,7... | collective-permute-start | bytes 1572872 | tf_op jit(solution)/shard_map/ppermute | solution.py:12
  23.3 9.5 %collective-permute-start.1 = (f32[16,64,128]{2,1,0:T(8,128)S(1)}, f32[16,64,128]{2,1,0:T(8,128)S(1)}, u32[]{:S(2)}, u32[]{:S(2)}) collective-permute-start(f32[16,64,128]{2,1,0:T(8,128)S(1)} %get-tuple-element.53), channel_id=1, source_target_pairs={{8,0},{16,8},{24,16},{32,24},{40,32},{48,40},{56,48},{64,56},{72,6... | collective-permute-start | bytes 1572872 | tf_op jit(solution)/shard_map/ppermute | solution.py:12
  32.8 9.9 %collective-permute-done = f32[16,64,128]{2,1,0:T(8,128)S(1)} collective-permute-done((f32[16,64,128]{2,1,0:T(8,128)S(1)}, f32[16,64,128]{2,1,0:T(8,128)S(1)}, u32[]{:S(2)}, u32[]{:S(2)}) %collective-permute-start) | collective-permute-done | bytes 524320 | tf_op jit(solution)/shard_map/ppermute | solution.py:12
  44.0 1.9 collective-permute-start.2
  45.9 6.5 %collective-permute-start.3 = (f32[16,64,128]{2,1,0:T(8,128)S(1)}, f32[16,64,128]{2,1,0:T(8,128)S(1)}, u32[]{:S(2)}, u32[]{:S(2)}) collective-permute-start(f32[16,64,128]{2,1,0:T(8,128)S(1)} %get-tuple-element.57), channel_id=1, source_target_pairs={{8,0},{16,8},{24,16},{32,24},{40,32},{48,40},{56,48},{64,56},{72,6... | collective-permute-start | bytes 1572872 | tf_op jit(solution)/shard_map/ppermute | solution.py:12
  52.4 9.0 %collective-permute-done.2 = f32[16,64,128]{2,1,0:T(8,128)S(1)} collective-permute-done((f32[16,64,128]{2,1,0:T(8,128)S(1)}, f32[16,64,128]{2,1,0:T(8,128)S(1)}, u32[]{:S(2)}, u32[]{:S(2)}) %collective-permute-start.2) | collective-permute-done | bytes 524320 | tf_op jit(solution)/shard_map/ppermute | solution.py:12
  62.8 1.9 collective-permute-start.4
  64.7 6.5 %collective-permute-start.5 = (f32[16,64,128]{2,1,0:T(8,128)S(1)}, f32[16,64,128]{2,1,0:T(8,128)S(1)}, u32[]{:S(2)}, u32[]{:S(2)}) collective-permute-start(f32[16,64,128]{2,1,0:T(8,128)S(1)} %get-tuple-element.61), channel_id=1, source_target_pairs={{8,0},{16,8},{24,16},{32,24},{40,32},{48,40},{56,48},{64,56},{72,6... | collective-permute-start | bytes 1572872 | tf_op jit(solution)/shard_map/ppermute | solution.py:12
  71.2 8.1 %collective-permute-done.4 = f32[16,64,128]{2,1,0:T(8,128)S(1)} collective-permute-done((f32[16,64,128]{2,1,0:T(8,128)S(1)}, f32[16,64,128]{2,1,0:T(8,128)S(1)}, u32[]{:S(2)}, u32[]{:S(2)}) %collective-permute-start.4) | collective-permute-done | bytes 524320 | tf_op jit(solution)/shard_map/ppermute | solution.py:12
  82.6 6.5 %collective-permute-start.7 = (f32[16,64,128]{2,1,0:T(8,128)S(1)}, f32[16,64,128]{2,1,0:T(8,128)S(1)}, u32[]{:S(2)}, u32[]{:S(2)}) collective-permute-start(f32[16,64,128]{2,1,0:T(8,128)S(1)} %get-tuple-element.65), channel_id=1, source_target_pairs={{8,0},{16,8},{24,16},{32,24},{40,32},{48,40},{56,48},{64,56},{72,6... | collective-permute-start | bytes 1572872 | tf_op jit(solution)/shard_map/ppermute | solution.py:12
  89.1 7.2 %collective-permute-done.6 = f32[16,64,128]{2,1,0:T(8,128)S(1)} collective-permute-done((f32[16,64,128]{2,1,0:T(8,128)S(1)}, f32[16,64,128]{2,1,0:T(8,128)S(1)}, u32[]{:S(2)}, u32[]{:S(2)}) %collective-permute-start.6) | collective-permute-done | bytes 524320 | tf_op jit(solution)/shard_map/ppermute | solution.py:12
  99.5 6.5 %collective-permute-start.9 = (f32[16,64,128]{2,1,0:T(8,128)S(1)}, f32[16,64,128]{2,1,0:T(8,128)S(1)}, u32[]{:S(2)}, u32[]{:S(2)}) collective-permute-start(f32[16,64,128]{2,1,0:T(8,128)S(1)} %get-tuple-element.69), channel_id=1, source_target_pairs={{8,0},{16,8},{24,16},{32,24},{40,32},{48,40},{56,48},{64,56},{72,6... | collective-permute-start | bytes 1572872 | tf_op jit(solution)/shard_map/ppermute | solution.py:12
  106.0 6.2 %collective-permute-done.8 = f32[16,64,128]{2,1,0:T(8,128)S(1)} collective-permute-done((f32[16,64,128]{2,1,0:T(8,128)S(1)}, f32[16,64,128]{2,1,0:T(8,128)S(1)}, u32[]{:S(2)}, u32[]{:S(2)}) %collective-permute-start.8) | collective-permute-done | bytes 524320 | tf_op jit(solution)/shard_map/ppermute | solution.py:12
  115.6 6.5 %collective-permute-start.11 = (f32[16,64,128]{2,1,0:T(8,128)S(1)}, f32[16,64,128]{2,1,0:T(8,128)S(1)}, u32[]{:S(2)}, u32[]{:S(2)}) collective-permute-start(f32[16,64,128]{2,1,0:T(8,128)S(1)} %get-tuple-element.73), channel_id=1, source_target_pairs={{8,0},{16,8},{24,16},{32,24},{40,32},{48,40},{56,48},{64,56},{72,6... | collective-permute-start | bytes 1572872 | tf_op jit(solution)/shard_map/ppermute | solution.py:12
  122.1 5.3 %collective-permute-done.10 = f32[16,64,128]{2,1,0:T(8,128)S(1)} collective-permute-done((f32[16,64,128]{2,1,0:T(8,128)S(1)}, f32[16,64,128]{2,1,0:T(8,128)S(1)}, u32[]{:S(2)}, u32[]{:S(2)}) %collective-permute-start.10) | collective-permute-done | bytes 524320 | tf_op jit(solution)/shard_map/ppermute | solution.py:12
  130.8 6.5 %collective-permute-start.13 = (f32[16,64,128]{2,1,0:T(8,128)S(1)}, f32[16,64,128]{2,1,0:T(8,128)S(1)}, u32[]{:S(2)}, u32[]{:S(2)}) collective-permute-start(f32[16,64,128]{2,1,0:T(8,128)S(1)} %get-tuple-element.77), channel_id=1, source_target_pairs={{8,0},{16,8},{24,16},{32,24},{40,32},{48,40},{56,48},{64,56},{72,6... | collective-permute-start | bytes 1572872 | tf_op jit(solution)/shard_map/ppermute | solution.py:12
  137.3 5.2 %collective-permute-done.12 = f32[16,64,128]{2,1,0:T(8,128)S(1)} collective-permute-done((f32[16,64,128]{2,1,0:T(8,128)S(1)}, f32[16,64,128]{2,1,0:T(8,128)S(1)}, u32[]{:S(2)}, u32[]{:S(2)}) %collective-permute-start.12) | collective-permute-done | bytes 524320 | tf_op jit(solution)/shard_map/ppermute | solution.py:12
  146.1 6.5 %collective-permute-start.15 = (f32[16,64,128]{2,1,0:T(8,128)S(1)}, f32[16,64,128]{2,1,0:T(8,128)S(1)}, u32[]{:S(2)}, u32[]{:S(2)}) collective-permute-start(f32[16,64,128]{2,1,0:T(8,128)S(1)} %get-tuple-element.81), channel_id=1, source_target_pairs={{8,0},{16,8},{24,16},{32,24},{40,32},{48,40},{56,48},{64,56},{72,6... | collective-permute-start | bytes 1572872 | tf_op jit(solution)/shard_map/ppermute | solution.py:12
  152.6 5.2 %collective-permute-done.14 = f32[16,64,128]{2,1,0:T(8,128)S(1)} collective-permute-done((f32[16,64,128]{2,1,0:T(8,128)S(1)}, f32[16,64,128]{2,1,0:T(8,128)S(1)}, u32[]{:S(2)}, u32[]{:S(2)}) %collective-permute-start.14) | collective-permute-done | bytes 524320 | tf_op jit(solution)/shard_map/ppermute | solution.py:12
  161.4 6.5 %collective-permute-start.17 = (f32[16,64,128]{2,1,0:T(8,128)S(1)}, f32[16,64,128]{2,1,0:T(8,128)S(1)}, u32[]{:S(2)}, u32[]{:S(2)}) collective-permute-start(f32[16,64,128]{2,1,0:T(8,128)S(1)} %get-tuple-element.85), channel_id=1, source_target_pairs={{8,0},{16,8},{24,16},{32,24},{40,32},{48,40},{56,48},{64,56},{72,6... | collective-permute-start | bytes 1572872 | tf_op jit(solution)/shard_map/ppermute | solution.py:12
  167.9 5.6 %collective-permute-done.16 = f32[16,64,128]{2,1,0:T(8,128)S(1)} collective-permute-done((f32[16,64,128]{2,1,0:T(8,128)S(1)}, f32[16,64,128]{2,1,0:T(8,128)S(1)}, u32[]{:S(2)}, u32[]{:S(2)}) %collective-permute-start.16) | collective-permute-done | bytes 524320 | tf_op jit(solution)/shard_map/ppermute | solution.py:12
  177.4 6.5 %collective-permute-start.19 = (f32[16,64,128]{2,1,0:T(8,128)S(1)}, f32[16,64,128]{2,1,0:T(8,128)S(1)}, u32[]{:S(2)}, u32[]{:S(2)}) collective-permute-start(f32[16,64,128]{2,1,0:T(8,128)S(1)} %get-tuple-element.89), channel_id=1, source_target_pairs={{8,0},{16,8},{24,16},{32,24},{40,32},{48,40},{56,48},{64,56},{72,6... | collective-permute-start | bytes 1572872 | tf_op jit(solution)/shard_map/ppermute | solution.py:12
  183.9 6.7 %collective-permute-done.18 = f32[16,64,128]{2,1,0:T(8,128)S(1)} collective-permute-done((f32[16,64,128]{2,1,0:T(8,128)S(1)}, f32[16,64,128]{2,1,0:T(8,128)S(1)}, u32[]{:S(2)}, u32[]{:S(2)}) %collective-permute-start.18) | collective-permute-done | bytes 524320 | tf_op jit(solution)/shard_map/ppermute | solution.py:12
  192.5 2.5 collective-permute-start.20
  194.9 6.0 %collective-permute-start.21 = (f32[16,64,128]{2,1,0:T(8,128)S(1)}, f32[16,64,128]{2,1,0:T(8,128)S(1)}, u32[]{:S(2)}, u32[]{:S(2)}) collective-permute-start(f32[16,64,128]{2,1,0:T(8,128)S(1)} %get-tuple-element.93), channel_id=1, source_target_pairs={{8,0},{16,8},{24,16},{32,24},{40,32},{48,40},{56,48},{64,56},{72,6... | collective-permute-start | bytes 1572872 | tf_op jit(solution)/shard_map/ppermute | solution.py:12
  202.7 5.0 %collective-permute-done.20 = f32[16,64,128]{2,1,0:T(8,128)S(1)} collective-permute-done((f32[16,64,128]{2,1,0:T(8,128)S(1)}, f32[16,64,128]{2,1,0:T(8,128)S(1)}, u32[]{:S(2)}, u32[]{:S(2)}) %collective-permute-start.20) | collective-permute-done | bytes 524320 | tf_op jit(solution)/shard_map/ppermute | solution.py:12
  207.7 1.9 collective-permute-done.21
  210.6 4.1 %collective-permute-start.22 = (f32[16,64,128]{2,1,0:T(8,128)}, f32[16,64,128]{2,1,0:T(8,128)S(1)}, u32[]{:S(2)}, u32[]{:S(2)}) collective-permute-start(f32[16,64,128]{2,1,0:T(8,128)} %get-tuple-element.96), channel_id=1, source_target_pairs={{0,8},{8,16},{16,24},{24,32},{32,40},{40,48},{48,56},{56,64},{64,7... | collective-permute-start | bytes 1572872 | tf_op jit(solution)/shard_map/ppermute | solution.py:12
  214.7 4.5 %collective-permute-start.23 = (f32[16,64,128]{2,1,0:T(8,128)S(1)}, f32[16,64,128]{2,1,0:T(8,128)S(1)}, u32[]{:S(2)}, u32[]{:S(2)}) collective-permute-start(f32[16,64,128]{2,1,0:T(8,128)S(1)} %get-tuple-element.97), channel_id=1, source_target_pairs={{8,0},{16,8},{24,16},{32,24},{40,32},{48,40},{56,48},{64,56},{72,6... | collective-permute-start | bytes 1572872 | tf_op jit(solution)/shard_map/ppermute | solution.py:12
  221.5 2.9 %collective-permute-done.22 = f32[16,64,128]{2,1,0:T(8,128)S(1)} collective-permute-done((f32[16,64,128]{2,1,0:T(8,128)}, f32[16,64,128]{2,1,0:T(8,128)S(1)}, u32[]{:S(2)}, u32[]{:S(2)}) %collective-permute-start.22) | collective-permute-done | bytes 524320 | tf_op jit(solution)/shard_map/ppermute | solution.py:12
  235.2 27.7 %reduce-scatter.2.cloned.1.call-done = f32[2,16,128]{2,1,0:T(8,128)} async-done(((f32[2,128,128]{2,1,0:T(8,128)}), f32[2,16,128]{2,1,0:T(8,128)}) %reduce-scatter.2.cloned.1.call-update) | async-done | bytes 16400 | tf_op jit(solution)/shard_map/reduce_scatter | solution.py:89
  (85 shorter events, 53.5 us)
Async XLA Ops:
  7.2 9.6 %copy-start.1 = (bf16[128,1024]{1,0:T(8,128)(2,1)S(1)}, bf16[128,1024]{1,0:T(8,128)(2,1)}, u32[]{:S(2)}) copy-start(bf16[128,1024]{1,0:T(8,128)(2,1)} %param.8) | copy-start | bytes 786436
  8.6 10.1 %all-to-all-start = ((bf16[8,2,16,128]{3,2,1,0:T(8,128)(2,1)}), bf16[8,2,16,128]{3,2,1,0:T(8,128)(2,1)S(1)}, u32[]{:S(2)}, u32[]{:S(2)}) async-start(bf16[8,2,16,128]{3,2,1,0:T(8,128)(2,1)} %stack.32), calls=%async_computation | async-start | bytes 131072 | tf_op jit(solution)/shard_map/all_to_all | solution.py:20
  13.0 249.8 %reduce-scatter.2.cloned.1.call-start = ((), (), s32[]{:S(2)}) async-start(), calls=%async_computation.2 | async-start | bytes 147456 | tf_op jit(solution)/shard_map/reduce_scatter | solution.py:89
  13.9 0.7 copy-start.3
  14.0 1.9 copy-start
  15.3 0.7 copy-start.4
  16.8 1.0 copy-start.2
  19.5 23.2 %collective-permute-start = (f32[16,64,128]{2,1,0:T(8,128)S(1)}, f32[16,64,128]{2,1,0:T(8,128)S(1)}, u32[]{:S(2)}, u32[]{:S(2)}) collective-permute-start(f32[16,64,128]{2,1,0:T(8,128)S(1)} %get-tuple-element.52), channel_id=1, source_target_pairs={{0,8},{8,16},{16,24},{24,32},{32,40},{40,48},{48,56},{56,64},{64,7... | collective-permute-start | bytes 1572872 | tf_op jit(solution)/shard_map/ppermute | solution.py:12
  23.3 20.5 %collective-permute-start.1 = (f32[16,64,128]{2,1,0:T(8,128)S(1)}, f32[16,64,128]{2,1,0:T(8,128)S(1)}, u32[]{:S(2)}, u32[]{:S(2)}) collective-permute-start(f32[16,64,128]{2,1,0:T(8,128)S(1)} %get-tuple-element.53), channel_id=1, source_target_pairs={{8,0},{16,8},{24,16},{32,24},{40,32},{48,40},{56,48},{64,56},{72,6... | collective-permute-start | bytes 1572872 | tf_op jit(solution)/shard_map/ppermute | solution.py:12
  44.0 17.4 %collective-permute-start.2 = (f32[16,64,128]{2,1,0:T(8,128)S(1)}, f32[16,64,128]{2,1,0:T(8,128)S(1)}, u32[]{:S(2)}, u32[]{:S(2)}) collective-permute-start(f32[16,64,128]{2,1,0:T(8,128)S(1)} %get-tuple-element.56), channel_id=1, source_target_pairs={{0,8},{8,16},{16,24},{24,32},{32,40},{40,48},{48,56},{56,64},{64,7... | collective-permute-start | bytes 1572872 | tf_op jit(solution)/shard_map/ppermute | solution.py:12
  45.9 16.7 %collective-permute-start.3 = (f32[16,64,128]{2,1,0:T(8,128)S(1)}, f32[16,64,128]{2,1,0:T(8,128)S(1)}, u32[]{:S(2)}, u32[]{:S(2)}) collective-permute-start(f32[16,64,128]{2,1,0:T(8,128)S(1)} %get-tuple-element.57), channel_id=1, source_target_pairs={{8,0},{16,8},{24,16},{32,24},{40,32},{48,40},{56,48},{64,56},{72,6... | collective-permute-start | bytes 1572872 | tf_op jit(solution)/shard_map/ppermute | solution.py:12
  62.8 16.5 %collective-permute-start.4 = (f32[16,64,128]{2,1,0:T(8,128)S(1)}, f32[16,64,128]{2,1,0:T(8,128)S(1)}, u32[]{:S(2)}, u32[]{:S(2)}) collective-permute-start(f32[16,64,128]{2,1,0:T(8,128)S(1)} %get-tuple-element.60), channel_id=1, source_target_pairs={{0,8},{8,16},{16,24},{24,32},{32,40},{40,48},{48,56},{56,64},{64,7... | collective-permute-start | bytes 1572872 | tf_op jit(solution)/shard_map/ppermute | solution.py:12
  64.7 15.8 %collective-permute-start.5 = (f32[16,64,128]{2,1,0:T(8,128)S(1)}, f32[16,64,128]{2,1,0:T(8,128)S(1)}, u32[]{:S(2)}, u32[]{:S(2)}) collective-permute-start(f32[16,64,128]{2,1,0:T(8,128)S(1)} %get-tuple-element.61), channel_id=1, source_target_pairs={{8,0},{16,8},{24,16},{32,24},{40,32},{48,40},{56,48},{64,56},{72,6... | collective-permute-start | bytes 1572872 | tf_op jit(solution)/shard_map/ppermute | solution.py:12
  80.7 15.6 %collective-permute-start.6 = (f32[16,64,128]{2,1,0:T(8,128)S(1)}, f32[16,64,128]{2,1,0:T(8,128)S(1)}, u32[]{:S(2)}, u32[]{:S(2)}) collective-permute-start(f32[16,64,128]{2,1,0:T(8,128)S(1)} %get-tuple-element.64), channel_id=1, source_target_pairs={{0,8},{8,16},{16,24},{24,32},{32,40},{40,48},{48,56},{56,64},{64,7... | collective-permute-start | bytes 1572872 | tf_op jit(solution)/shard_map/ppermute | solution.py:12
  82.6 14.8 %collective-permute-start.7 = (f32[16,64,128]{2,1,0:T(8,128)S(1)}, f32[16,64,128]{2,1,0:T(8,128)S(1)}, u32[]{:S(2)}, u32[]{:S(2)}) collective-permute-start(f32[16,64,128]{2,1,0:T(8,128)S(1)} %get-tuple-element.65), channel_id=1, source_target_pairs={{8,0},{16,8},{24,16},{32,24},{40,32},{48,40},{56,48},{64,56},{72,6... | collective-permute-start | bytes 1572872 | tf_op jit(solution)/shard_map/ppermute | solution.py:12
  97.6 14.7 %collective-permute-start.8 = (f32[16,64,128]{2,1,0:T(8,128)S(1)}, f32[16,64,128]{2,1,0:T(8,128)S(1)}, u32[]{:S(2)}, u32[]{:S(2)}) collective-permute-start(f32[16,64,128]{2,1,0:T(8,128)S(1)} %get-tuple-element.68), channel_id=1, source_target_pairs={{0,8},{8,16},{16,24},{24,32},{32,40},{40,48},{48,56},{56,64},{64,7... | collective-permute-start | bytes 1572872 | tf_op jit(solution)/shard_map/ppermute | solution.py:12
  99.5 13.9 %collective-permute-start.9 = (f32[16,64,128]{2,1,0:T(8,128)S(1)}, f32[16,64,128]{2,1,0:T(8,128)S(1)}, u32[]{:S(2)}, u32[]{:S(2)}) collective-permute-start(f32[16,64,128]{2,1,0:T(8,128)S(1)} %get-tuple-element.69), channel_id=1, source_target_pairs={{8,0},{16,8},{24,16},{32,24},{40,32},{48,40},{56,48},{64,56},{72,6... | collective-permute-start | bytes 1572872 | tf_op jit(solution)/shard_map/ppermute | solution.py:12
  113.6 13.7 %collective-permute-start.10 = (f32[16,64,128]{2,1,0:T(8,128)S(1)}, f32[16,64,128]{2,1,0:T(8,128)S(1)}, u32[]{:S(2)}, u32[]{:S(2)}) collective-permute-start(f32[16,64,128]{2,1,0:T(8,128)S(1)} %get-tuple-element.72), channel_id=1, source_target_pairs={{0,8},{8,16},{16,24},{24,32},{32,40},{40,48},{48,56},{56,64},{64,7... | collective-permute-start | bytes 1572872 | tf_op jit(solution)/shard_map/ppermute | solution.py:12
  115.6 13.2 %collective-permute-start.11 = (f32[16,64,128]{2,1,0:T(8,128)S(1)}, f32[16,64,128]{2,1,0:T(8,128)S(1)}, u32[]{:S(2)}, u32[]{:S(2)}) collective-permute-start(f32[16,64,128]{2,1,0:T(8,128)S(1)} %get-tuple-element.73), channel_id=1, source_target_pairs={{8,0},{16,8},{24,16},{32,24},{40,32},{48,40},{56,48},{64,56},{72,6... | collective-permute-start | bytes 1572872 | tf_op jit(solution)/shard_map/ppermute | solution.py:12
  128.9 13.7 %collective-permute-start.12 = (f32[16,64,128]{2,1,0:T(8,128)S(1)}, f32[16,64,128]{2,1,0:T(8,128)S(1)}, u32[]{:S(2)}, u32[]{:S(2)}) collective-permute-start(f32[16,64,128]{2,1,0:T(8,128)S(1)} %get-tuple-element.76), channel_id=1, source_target_pairs={{0,8},{8,16},{16,24},{24,32},{32,40},{40,48},{48,56},{56,64},{64,7... | collective-permute-start | bytes 1572872 | tf_op jit(solution)/shard_map/ppermute | solution.py:12
  130.8 13.2 %collective-permute-start.13 = (f32[16,64,128]{2,1,0:T(8,128)S(1)}, f32[16,64,128]{2,1,0:T(8,128)S(1)}, u32[]{:S(2)}, u32[]{:S(2)}) collective-permute-start(f32[16,64,128]{2,1,0:T(8,128)S(1)} %get-tuple-element.77), channel_id=1, source_target_pairs={{8,0},{16,8},{24,16},{32,24},{40,32},{48,40},{56,48},{64,56},{72,6... | collective-permute-start | bytes 1572872 | tf_op jit(solution)/shard_map/ppermute | solution.py:12
  144.2 13.7 %collective-permute-start.14 = (f32[16,64,128]{2,1,0:T(8,128)S(1)}, f32[16,64,128]{2,1,0:T(8,128)S(1)}, u32[]{:S(2)}, u32[]{:S(2)}) collective-permute-start(f32[16,64,128]{2,1,0:T(8,128)S(1)} %get-tuple-element.80), channel_id=1, source_target_pairs={{0,8},{8,16},{16,24},{24,32},{32,40},{40,48},{48,56},{56,64},{64,7... | collective-permute-start | bytes 1572872 | tf_op jit(solution)/shard_map/ppermute | solution.py:12
  146.1 13.2 %collective-permute-start.15 = (f32[16,64,128]{2,1,0:T(8,128)S(1)}, f32[16,64,128]{2,1,0:T(8,128)S(1)}, u32[]{:S(2)}, u32[]{:S(2)}) collective-permute-start(f32[16,64,128]{2,1,0:T(8,128)S(1)} %get-tuple-element.81), channel_id=1, source_target_pairs={{8,0},{16,8},{24,16},{32,24},{40,32},{48,40},{56,48},{64,56},{72,6... | collective-permute-start | bytes 1572872 | tf_op jit(solution)/shard_map/ppermute | solution.py:12
  159.5 14.0 %collective-permute-start.16 = (f32[16,64,128]{2,1,0:T(8,128)S(1)}, f32[16,64,128]{2,1,0:T(8,128)S(1)}, u32[]{:S(2)}, u32[]{:S(2)}) collective-permute-start(f32[16,64,128]{2,1,0:T(8,128)S(1)} %get-tuple-element.84), channel_id=1, source_target_pairs={{0,8},{8,16},{16,24},{24,32},{32,40},{40,48},{48,56},{56,64},{64,7... | collective-permute-start | bytes 1572872 | tf_op jit(solution)/shard_map/ppermute | solution.py:12
  161.4 13.8 %collective-permute-start.17 = (f32[16,64,128]{2,1,0:T(8,128)S(1)}, f32[16,64,128]{2,1,0:T(8,128)S(1)}, u32[]{:S(2)}, u32[]{:S(2)}) collective-permute-start(f32[16,64,128]{2,1,0:T(8,128)S(1)} %get-tuple-element.85), channel_id=1, source_target_pairs={{8,0},{16,8},{24,16},{32,24},{40,32},{48,40},{56,48},{64,56},{72,6... | collective-permute-start | bytes 1572872 | tf_op jit(solution)/shard_map/ppermute | solution.py:12
  175.4 15.1 %collective-permute-start.18 = (f32[16,64,128]{2,1,0:T(8,128)S(1)}, f32[16,64,128]{2,1,0:T(8,128)S(1)}, u32[]{:S(2)}, u32[]{:S(2)}) collective-permute-start(f32[16,64,128]{2,1,0:T(8,128)S(1)} %get-tuple-element.88), channel_id=1, source_target_pairs={{0,8},{8,16},{16,24},{24,32},{32,40},{40,48},{48,56},{56,64},{64,7... | collective-permute-start | bytes 1572872 | tf_op jit(solution)/shard_map/ppermute | solution.py:12
  177.4 14.9 %collective-permute-start.19 = (f32[16,64,128]{2,1,0:T(8,128)S(1)}, f32[16,64,128]{2,1,0:T(8,128)S(1)}, u32[]{:S(2)}, u32[]{:S(2)}) collective-permute-start(f32[16,64,128]{2,1,0:T(8,128)S(1)} %get-tuple-element.89), channel_id=1, source_target_pairs={{8,0},{16,8},{24,16},{32,24},{40,32},{48,40},{56,48},{64,56},{72,6... | collective-permute-start | bytes 1572872 | tf_op jit(solution)/shard_map/ppermute | solution.py:12
  192.5 15.2 %collective-permute-start.20 = (f32[16,64,128]{2,1,0:T(8,128)S(1)}, f32[16,64,128]{2,1,0:T(8,128)S(1)}, u32[]{:S(2)}, u32[]{:S(2)}) collective-permute-start(f32[16,64,128]{2,1,0:T(8,128)S(1)} %get-tuple-element.92), channel_id=1, source_target_pairs={{0,8},{8,16},{16,24},{24,32},{32,40},{40,48},{48,56},{56,64},{64,7... | collective-permute-start | bytes 1572872 | tf_op jit(solution)/shard_map/ppermute | solution.py:12
  194.9 14.7 %collective-permute-start.21 = (f32[16,64,128]{2,1,0:T(8,128)S(1)}, f32[16,64,128]{2,1,0:T(8,128)S(1)}, u32[]{:S(2)}, u32[]{:S(2)}) collective-permute-start(f32[16,64,128]{2,1,0:T(8,128)S(1)} %get-tuple-element.93), channel_id=1, source_target_pairs={{8,0},{16,8},{24,16},{32,24},{40,32},{48,40},{56,48},{64,56},{72,6... | collective-permute-start | bytes 1572872 | tf_op jit(solution)/shard_map/ppermute | solution.py:12
  210.6 13.8 %collective-permute-start.22 = (f32[16,64,128]{2,1,0:T(8,128)}, f32[16,64,128]{2,1,0:T(8,128)S(1)}, u32[]{:S(2)}, u32[]{:S(2)}) collective-permute-start(f32[16,64,128]{2,1,0:T(8,128)} %get-tuple-element.96), channel_id=1, source_target_pairs={{0,8},{8,16},{16,24},{24,32},{32,40},{40,48},{48,56},{56,64},{64,7... | collective-permute-start | bytes 1572872 | tf_op jit(solution)/shard_map/ppermute | solution.py:12
  214.7 11.1 %collective-permute-start.23 = (f32[16,64,128]{2,1,0:T(8,128)S(1)}, f32[16,64,128]{2,1,0:T(8,128)S(1)}, u32[]{:S(2)}, u32[]{:S(2)}) collective-permute-start(f32[16,64,128]{2,1,0:T(8,128)S(1)} %get-tuple-element.97), channel_id=1, source_target_pairs={{8,0},{16,8},{24,16},{32,24},{40,32},{48,40},{56,48},{64,56},{72,6... | collective-permute-start | bytes 1572872 | tf_op jit(solution)/shard_map/ppermute | solution.py:12
  228.9 0.7 copy-start.5
Sparse Core Ops, SparseCore 0:
  229.0 33.7 reduce-scatter.1
